TPU v7x, 128 devices: a whole 4x4x4 slice. The times are simulated.
128 devices in a mesh: lat: 8 (over y_lo, z), lon: 16 (over x, y_hi, core).
Axes of the slice: x: 4, y: 4 (y_hi: 2, y_lo: 2; y = y_hi * 2 + y_lo), z: 4, core: 2. Of those that a mesh axis runs over, the one named last changes fastest.
Arguments:
- starting_sea_elevation: float32 [256, 2048], P('lat', 'lon'), may hold values from -6 to 6
- zonal_integrated_flux: float32 [256, 2048], P('lat', 'lon'), may hold values from -6 to 6
- meridional_integrated_flux: float32 [256, 2048], P('lat', 'lon'), may hold values from -6 to 6
- ocean_strata_total: int32 [256, 2048], P('lat', 'lon'), may hold values from 0 to 8
- thermal_anomaly: float32 [8, 256, 2048], P(None, 'lat', 'lon'), may hold values from -6 to 6
- zonal_baroclinic_velocity: float32 [8, 256, 2048], P(None, 'lat', 'lon'), may hold values from -3 to 3
- meridional_baroclinic_velocity: float32 [8, 256, 2048], P(None, 'lat', 'lon'), may hold values from -3 to 3
- sent_sender_mesh_index: int32 [128, 128, 1024], P(('lat', 'lon')), may hold values from 0 to 4095
- sent_intersection_extent: float32 [128, 128, 1024], P(('lat', 'lon')), may hold values from 0.2 to 1
- sent_entry_tally: int32 [128, 128], P(('lat', 'lon')), may hold values from 0 to 1024, as said below
- received_atmosphere_mesh_index: int32 [128, 128, 1024], P(('lat', 'lon')), may hold values from 0 to 4095
Outputs:
- height_new: float32 [256, 2048], P('lat', 'lon')
- east_new: float32 [256, 2048], P('lat', 'lon')
- north_new: float32 [256, 2048], P('lat', 'lon')
- temperature_new: float32 [8, 256, 2048], P(None, 'lat', 'lon')
- atmosphere_fields: float32 [4, 524288], P(None, ('lat', 'lon'))
Inputs may be any that keep to these rules, and one draw needn't show every extreme that they name: Slots j >= sent_entry_tally[s, d] are unused. In every draw one owner receives exactly 1024 live slots from every device. `sent_sender_mesh_index`: A cell of the sending device's block, numbered row by row. `received_atmosphere_mesh_index`: an atmosphere cell of the receiving owner. `ocean_strata_total`: 0 is land.
All inputs are finite; a program needn't handle non-finite values.
Results may differ from a plain program's by a relative error of at most 0.00017.
Values sent between devices are 32-bit elements; how exact they have to be, the bound alone decides.
No kernel may reach another device: no remote copies, remote signals or barrier semaphores. Data moves between devices by JAX's collectives and lax.ppermute only.
A program may use at most 64 MiB of HBM per device.

v0:
```python
import math
import jax
import jax.numpy as jnp
from jax import lax
from jax.sharding import PartitionSpec as P

VERTICAL_STRATA = 8
STEPS = 4
NF = 4
ACELL = 4096
mass_coef = 0.7
slope_coef = 0.7
spin_coef = 0.3
mix_coef = 0.1
carry_coef = 0.1
block_limit = 8192


def with_halo(block, sides, width, periodic):
    for axis, dim in sides:
        count = lax.axis_size(axis)
        forward = [(i, i + 1) for i in range(count - 1)]
        if periodic:
            forward.append((count - 1, 0))
        backward = [(target, source) for source, target in forward]
        low = lax.ppermute(
            lax.slice_in_dim(block, block.shape[dim] - width, None, axis=dim), axis, forward
        )
        high = lax.ppermute(lax.slice_in_dim(block, 0, width, axis=dim), axis, backward)
        block = jnp.concatenate([low, block, high], axis=dim)
    return block


def widen(fields, signs, width):
    rows = fields.shape[1]
    lon_wide = with_halo(fields, (("lon", 2),), width, True)
    both_wide = with_halo(lon_wide, (("lat", 1),), width, False)
    upper = jnp.flip(lon_wide[:, rows - width :, :], axis=(1, 2))
    sectors = lax.axis_size("lon")
    collected = lax.all_gather(upper[None], "lon", axis=0, tiled=True)
    mirrored = lax.dynamic_index_in_dim(
        collected, sectors - 1 - lax.axis_index("lon"), 0, keepdims=False
    )
    folded = mirrored * signs[:, None, None]
    on_top = lax.axis_index("lat") == lax.axis_size("lat") - 1
    top_rim = jnp.where(on_top, folded, both_wide[:, rows + width :, :])
    return jnp.concatenate([both_wide[:, : rows + width, :], top_rim], axis=1)


def pick_cells(surface_grid, indices):
    fields_count, rows, columns = surface_grid.shape
    table = jnp.transpose(surface_grid, (2, 0, 1)).reshape(columns, fields_count * rows)
    total = indices.shape[0]
    size = math.gcd(total, block_limit)
    blocks = indices.reshape(total // size, size)
    column_ids = jnp.arange(columns)
    row_ids = jnp.arange(rows)

    def one_block(block):
        column_hot = (block[:, None] % columns == column_ids[None, :]).astype(jnp.float32)
        row_hot = (block[:, None] // columns == row_ids[None, :]).astype(jnp.float32)
        by_column = jnp.dot(
            column_hot, table, precision=lax.Precision.HIGHEST, preferred_element_type=jnp.float32
        )
        by_column = by_column.reshape(size, fields_count, rows)
        return jnp.sum(by_column * row_hot[:, None, :], axis=2)

    picked = lax.map(one_block, blocks).reshape(total, fields_count)
    return jnp.transpose(picked)


def spread_cells(values, targets, cells):
    fields_count = values.shape[0]
    total = targets.shape[0]
    size = math.gcd(total, block_limit)
    high_count = cells // 128
    value_blocks = jnp.transpose(values.reshape(fields_count, total // size, size), (1, 0, 2))
    target_blocks = targets.reshape(total // size, size)
    low_ids = jnp.arange(128)
    high_ids = jnp.arange(high_count)

    def add_block(carry, pieces):
        value_block, target_block = pieces
        low_hot = (target_block[:, None] % 128 == low_ids[None, :]).astype(jnp.float32)
        high_hot = (target_block[:, None] // 128 == high_ids[None, :]).astype(jnp.float32)
        weighted = (jnp.transpose(value_block)[:, :, None] * high_hot[:, None, :]).reshape(
            size, fields_count * high_count
        )
        term = lax.dot_general(
            weighted,
            low_hot,
            (((0,), (0,)), ((), ())),
            precision=lax.Precision.HIGHEST,
            preferred_element_type=jnp.float32,
        )
        return (carry + term, None)

    start = jnp.zeros((fields_count * high_count, 128), jnp.float32)
    summed, _ = lax.scan(add_block, start, (value_blocks, target_blocks))
    return summed.reshape(fields_count, cells)


def local(
    starting_sea_elevation,
    zonal_integrated_flux,
    meridional_integrated_flux,
    ocean_strata_total,
    thermal_anomaly,
    zonal_baroclinic_velocity,
    meridional_baroclinic_velocity,
    sent_sender_mesh_index,
    sent_intersection_extent,
    sent_entry_tally,
    received_atmosphere_mesh_index,
):
    band_rows = starting_sea_elevation.shape[0]
    grid_rows = band_rows * lax.axis_size("lat")
    band = lax.axis_index("lat")
    depth = ocean_strata_total.astype(jnp.float32)
    wet = (ocean_strata_total > 0).astype(jnp.float32)
    hnorm = depth / VERTICAL_STRATA
    height = starting_sea_elevation * wet
    east = zonal_integrated_flux * wet
    north = meridional_integrated_flux * wet
    rows = (band * band_rows + jnp.arange(band_rows)).astype(jnp.float32)
    rotation = (-spin_coef * jnp.cos(jnp.pi * (rows + 0.5) / grid_rows))[:, None]
    vector_signs = jnp.array([-1.0, -1.0], jnp.float32)
    scalar_signs = jnp.array([1.0], jnp.float32)
    for step in range(STEPS):
        moved = widen(jnp.stack([east, north]), vector_signs, 1)
        east_e = moved[0, 1:-1, 2:]
        east_w = moved[0, 1:-1, :-2]
        north_n = moved[1, 2:, 1:-1]
        north_s = moved[1, :-2, 1:-1]
        height = wet * (height - mass_coef * (east_e - east_w + (north_n - north_s)))
        height_wide = widen(height[None], scalar_signs, 1)[0]
        height_e = height_wide[1:-1, 2:]
        height_w = height_wide[1:-1, :-2]
        height_n = height_wide[2:, 1:-1]
        height_s = height_wide[:-2, 1:-1]
        east = wet * (east - slope_coef * hnorm * (height_e - height_w) + rotation * north)
        north = wet * (north - slope_coef * hnorm * (height_n - height_s) - rotation * east)
    levels_int = jnp.arange(VERTICAL_STRATA)[:, None, None]
    levels_float = jnp.arange(VERTICAL_STRATA).astype(jnp.float32)[:, None, None]
    submerged_stratum_mask = (levels_int < ocean_strata_total[None]).astype(jnp.float32)
    passive_scalar_values = thermal_anomaly * submerged_stratum_mask
    tracer_signs = jnp.ones((VERTICAL_STRATA + 1,), jnp.float32)
    widened = widen(jnp.concatenate([passive_scalar_values, depth[None]], axis=0), tracer_signs, 1)
    tracer_wide = widened[:VERTICAL_STRATA]
    wet_wide = (levels_float < widened[VERTICAL_STRATA][None]).astype(jnp.float32)
    tracer_e = tracer_wide[:, 1:-1, 2:]
    tracer_w = tracer_wide[:, 1:-1, :-2]
    tracer_n = tracer_wide[:, 2:, 1:-1]
    tracer_s = tracer_wide[:, :-2, 1:-1]
    wet_e = wet_wide[:, 1:-1, 2:]
    wet_w = wet_wide[:, 1:-1, :-2]
    wet_n = wet_wide[:, 2:, 1:-1]
    wet_s = wet_wide[:, :-2, 1:-1]
    mixing = (
        wet_e * (tracer_e - passive_scalar_values)
        + wet_w * (tracer_w - passive_scalar_values)
        + wet_n * (tracer_n - passive_scalar_values)
        + wet_s * (tracer_s - passive_scalar_values)
    )
    speed_east = east[None] + zonal_baroclinic_velocity
    speed_north = north[None] + meridional_baroclinic_velocity
    carried = speed_east * (tracer_e - tracer_w) + speed_north * (tracer_n - tracer_s)
    tracer_new = submerged_stratum_mask * (
        passive_scalar_values + mix_coef * mixing - carry_coef * carried
    )
    surface_grid = jnp.stack([height, speed_east[0], speed_north[0], tracer_new[0]])
    owners = sent_sender_mesh_index.shape[1]
    slots = sent_sender_mesh_index.shape[2]
    picked = pick_cells(surface_grid, sent_sender_mesh_index[0].reshape(-1)).reshape(
        NF, owners, slots
    )
    live = jnp.arange(slots)[None, :] < sent_entry_tally[0][:, None]
    values = jnp.where(live[None], sent_intersection_extent[0][None] * picked, 0.0)
    targets = received_atmosphere_mesh_index[0].reshape(-1)
    block = lax.all_to_all(values, ("lat", "lon"), split_axis=1, concat_axis=1, tiled=True)
    fields_count = block.shape[0]
    atmosphere = spread_cells(block.reshape(fields_count, -1), targets, ACELL)
    return (height, east, north, tracer_new, atmosphere)


def solution(mesh):
    in_specs = (
        P("lat", "lon"),
        P("lat", "lon"),
        P("lat", "lon"),
        P("lat", "lon"),
        P(None, "lat", "lon"),
        P(None, "lat", "lon"),
        P(None, "lat", "lon"),
        P(("lat", "lon"), None, None),
        P(("lat", "lon"), None, None),
        P(("lat", "lon"), None),
        P(("lat", "lon"), None, None),
    )
    out_specs = (
        P("lat", "lon"),
        P("lat", "lon"),
        P("lat", "lon"),
        P(None, "lat", "lon"),
        P(None, ("lat", "lon")),
    )
    return jax.shard_map(local, mesh=mesh, in_specs=in_specs, out_specs=out_specs, check_vma=False)
```

profile of v0, /device:TPU:1, one launch (start us, length us, event | category | flops | bytes accessed | tf_op | source)
XLA Modules:
  0.0 557.0 jit_solution(9308671634009213808)
XLA Ops:
  19.4 24.9 %all-gather = f32[32,1,130]{2,1,0:T(1,128)S(1)} all-gather(f32[2,1,130]{2,1,0:T(1,128)S(1)} %slice.507), channel_id=2, replica_groups=mesh['lat'=8,'lon'=16] {'lon'}, dimensions={0}, use_global_device_ids=true | all-gather | bytes 17680 | tf_op jit(solution)/shard_map/all_gather | solution.py:40
  58.0 19.8 %all-gather.1 = f32[16,1,130]{2,1,0:T(1,128)S(1)} all-gather(f32[1,1,130]{2,1,0:T(1,128)S(1)} %slice.508), channel_id=3, replica_groups=mesh['lat'=8,'lon'=16] {'lon'}, dimensions={0}, use_global_device_ids=true | all-gather | bytes 8840 | tf_op jit(solution)/shard_map/all_gather | solution.py:40
  91.5 20.9 %all-gather.2 = f32[32,1,130]{2,1,0:T(1,128)S(1)} all-gather(f32[2,1,130]{2,1,0:T(1,128)S(1)} %slice.509), channel_id=4, replica_groups=mesh['lat'=8,'lon'=16] {'lon'}, dimensions={0}, use_global_device_ids=true | all-gather | bytes 17680 | tf_op jit(solution)/shard_map/all_gather | solution.py:40
  126.5 19.5 %all-gather.3 = f32[16,1,130]{2,1,0:T(1,128)S(1)} all-gather(f32[1,1,130]{2,1,0:T(1,128)S(1)} %slice.510), channel_id=5, replica_groups=mesh['lat'=8,'lon'=16] {'lon'}, dimensions={0}, use_global_device_ids=true | all-gather | bytes 8840 | tf_op jit(solution)/shard_map/all_gather | solution.py:40
  149.6 19.8 %all-gather.8 = f32[144,1,130]{2,1,0:T(1,128)S(1)} all-gather(f32[9,1,130]{2,1,0:T(1,128)S(1)} %slice.515), channel_id=10, replica_groups=mesh['lat'=8,'lon'=16] {'lon'}, dimensions={0}, use_global_device_ids=true | all-gather | bytes 79560 | tf_op jit(solution)/shard_map/all_gather | solution.py:40
  169.5 6.1 %collective-permute-start.19 = (f32[2,1,130]{2,1,0:T(1,128)S(1)}, f32[2,1,130]{2,1,0:T(1,128)}, u32[]{:S(2)}, u32[]{:S(2)}) collective-permute-start(f32[2,1,130]{2,1,0:T(1,128)S(1)} %get-tuple-element.265), channel_id=1, source_target_pairs={{0,16},{16,32},{32,48},{48,64},{64,80},{80,96},{96,112},{1,17},{17... | collective-permute-start | bytes 3128 | tf_op jit(solution)/shard_map/ppermute | solution.py:26
  177.1 21.3 %all-gather.4 = f32[32,1,130]{2,1,0:T(1,128)S(1)} all-gather(f32[2,1,130]{2,1,0:T(1,128)S(1)} %slice.511), channel_id=6, replica_groups=mesh['lat'=8,'lon'=16] {'lon'}, dimensions={0}, use_global_device_ids=true | all-gather | bytes 17680 | tf_op jit(solution)/shard_map/all_gather | solution.py:40
  211.7 20.9 %all-gather.5 = f32[16,1,130]{2,1,0:T(1,128)S(1)} all-gather(f32[1,1,130]{2,1,0:T(1,128)S(1)} %slice.512), channel_id=7, replica_groups=mesh['lat'=8,'lon'=16] {'lon'}, dimensions={0}, use_global_device_ids=true | all-gather | bytes 8840 | tf_op jit(solution)/shard_map/all_gather | solution.py:40
  238.6 6.4 %collective-permute-start.27 = (f32[2,1,130]{2,1,0:T(1,128)S(1)}, f32[2,1,130]{2,1,0:T(1,128)S(1)}, u32[]{:S(2)}, u32[]{:S(2)}) collective-permute-start(f32[2,1,130]{2,1,0:T(1,128)S(1)} %get-tuple-element.263), channel_id=1, source_target_pairs={{0,16},{16,32},{32,48},{48,64},{64,80},{80,96},{96,112},{1,17},{17... | collective-permute-start | bytes 3128 | tf_op jit(solution)/shard_map/ppermute | solution.py:26
  246.5 24.1 %all-gather.6 = f32[32,1,130]{2,1,0:T(1,128)S(1)} all-gather(f32[2,1,130]{2,1,0:T(1,128)S(1)} %slice.513), channel_id=8, replica_groups=mesh['lat'=8,'lon'=16] {'lon'}, dimensions={0}, use_global_device_ids=true | all-gather | bytes 17680 | tf_op jit(solution)/shard_map/all_gather | solution.py:40
  280.1 7.1 %collective-permute-start.30 = (f32[1,1,130]{2,1,0:T(1,128)}, f32[1,1,130]{2,1,0:T(1,128)}, u32[]{:S(2)}, u32[]{:S(2)}) collective-permute-start(f32[1,1,130]{2,1,0:T(1,128)} %get-tuple-element.270), channel_id=1, source_target_pairs={{0,16},{16,32},{32,48},{48,64},{64,80},{80,96},{96,112},{1,17},{17... | collective-permute-start | bytes 1568 | tf_op jit(solution)/shard_map/ppermute | solution.py:26
  290.7 19.7 %all-gather.7 = f32[16,1,130]{2,1,0:T(1,128)S(1)} all-gather(f32[1,1,130]{2,1,0:T(1,128)S(1)} %slice.514), channel_id=9, replica_groups=mesh['lat'=8,'lon'=16] {'lon'}, dimensions={0}, use_global_device_ids=true | all-gather | bytes 8840 | tf_op jit(solution)/shard_map/all_gather | solution.py:40
  314.2 62.9 %while.26 = (s32[]{:T(128)}, f32[16,8192,4]{1,2,0:T(4,128)S(1)}, s32[16,8192]{1,0:T(8,128)S(1)}, f32[128,128]{1,0:T(8,128)S(1)}, s32[]{:T(128)}) while((s32[]{:T(128)}, f32[16,8192,4]{1,2,0:T(4,128)S(1)}, s32[16,8192]{1,0:T(8,128)S(1)}, f32[128,128]{1,0:T(8,128)S(1)}, s32[]{:T(128)}) %tuple.96), condition=%wide.region_2.3_spmd.clone, body=%wide.region_0.2_spmd.clone.sunk | while | flops 1614405632 | bytes 2785349 | solution.py:68
  382.2 14.8 %all-to-all-start = ((f32[4,128,1024]{2,0,1:T(4,128)}), f32[4,128,1024]{2,0,1:T(4,128)S(1)}, u32[]{:S(2)}, u32[]{:S(2)}) async-start(f32[4,128,1024]{2,0,1:T(4,128)} %copy.26), calls=%async_computation | async-start | bytes 4194304 | tf_op jit(solution)/shard_map/all_to_all | solution.py:180
  398.1 29.0 %all-to-all-done = f32[4,128,1024]{2,0,1:T(4,128)S(1)} async-done(((f32[4,128,1024]{2,0,1:T(4,128)}), f32[4,128,1024]{2,0,1:T(4,128)S(1)}, u32[]{:S(2)}, u32[]{:S(2)}) %all-to-all-start) | async-done | bytes 2097184 | tf_op jit(solution)/shard_map/all_to_all | solution.py:180
  431.5 124.9 %while.27 = (s32[]{:T(128)}, f32[128,128]{1,0:T(8,128)S(1)}, f32[16,4,8192]{2,0,1:T(8,128)S(1)}, s32[16,8192]{1,0:T(8,128)S(1)}, s32[]{:T(128)}, /*index=5*/s32[]{:T(128)}) while((s32[]{:T(128)}, f32[128,128]{1,0:T(8,128)S(1)}, f32[16,4,8192]{2,0,1:T(8,128)S(1)}, s32[16,8192]{1,0:T(8,128)S(1)}, s32[]{:T(128)}, ...), condition=%wide.region_4.5_spmd.clone, body=%wide.region_3.4_spmd.clone.sunk | while | flops 1613422592 | bytes 11501655 | solution.py:99
  434.3 5.0 fusion.118
  442.1 5.0 fusion.118
  449.9 5.0 fusion.118
  457.7 5.0 fusion.118
  465.5 5.0 fusion.118
  473.3 5.0 fusion.118
  481.1 5.0 fusion.118
  488.9 5.0 fusion.118
  496.7 5.0 fusion.118
  504.5 5.0 fusion.118
  512.3 5.0 fusion.118
  520.1 5.0 fusion.118
  528.0 5.0 fusion.118
  535.8 5.0 fusion.118
  543.6 5.0 fusion.118
  551.4 5.0 fusion.118
  (358 shorter events, 219.9 us)
Async XLA Ops:
  2.9 11.3 %collective-permute-start = (f32[2,32,1]{2,1,0:T(8,128)}, f32[2,32,1]{2,1,0:T(8,128)S(1)}, u32[]{:S(2)}, u32[]{:S(2)}) collective-permute-start(f32[2,32,1]{2,1,0:T(8,128)} %get-tuple-element.285), channel_id=1, source_target_pairs={{1,0},{2,1},{3,2},{4,3},{5,4},{6,5},{7,6},{8,7},{9,8},{10,9},{11,1... | collective-permute-start | bytes 776 | tf_op jit(solution)/shard_map/ppermute | solution.py:29
  4.2 9.9 %collective-permute-start.1 = (f32[2,32,1]{2,1,0:T(8,128)}, f32[2,32,1]{2,1,0:T(8,128)S(1)}, u32[]{:S(2)}, u32[]{:S(2)}) collective-permute-start(f32[2,32,1]{2,1,0:T(8,128)} %get-tuple-element.284), channel_id=1, source_target_pairs={{0,1},{1,2},{2,3},{3,4},{4,5},{5,6},{6,7},{7,8},{8,9},{9,10},{10,1... | collective-permute-start | bytes 776 | tf_op jit(solution)/shard_map/ppermute | solution.py:26
  9.6 37.8 %collective-permute-start.32 = (f32[9,32,1]{2,1,0:T(8,128)}, f32[9,32,1]{2,1,0:T(8,128)S(1)}, u32[]{:S(2)}, u32[]{:S(2)}) collective-permute-start(f32[9,32,1]{2,1,0:T(8,128)} %get-tuple-element.260), channel_id=1, source_target_pairs={{0,1},{1,2},{2,3},{3,4},{4,5},{5,6},{6,7},{7,8},{8,9},{9,10},{10,1... | collective-permute-start | bytes 3464 | tf_op jit(solution)/shard_map/ppermute | solution.py:26
  10.1 37.3 %collective-permute-start.33 = (f32[9,32,1]{2,1,0:T(8,128)S(1)}, f32[9,32,1]{2,1,0:T(8,128)S(1)}, u32[]{:S(2)}, u32[]{:S(2)}) collective-permute-start(f32[9,32,1]{2,1,0:T(8,128)S(1)} %get-tuple-element.261), channel_id=1, source_target_pairs={{1,0},{2,1},{3,2},{4,3},{5,4},{6,5},{7,6},{8,7},{9,8},{10,9},{11,1... | collective-permute-start | bytes 3464 | tf_op jit(solution)/shard_map/ppermute | solution.py:29
  14.3 30.0 %collective-permute-start.3 = (f32[2,1,130]{2,1,0:T(1,128)S(1)}, f32[2,1,130]{2,1,0:T(1,128)S(1)}, u32[]{:S(2)}, u32[]{:S(2)}) collective-permute-start(f32[2,1,130]{2,1,0:T(1,128)S(1)} %get-tuple-element.269), channel_id=1, source_target_pairs={{0,16},{16,32},{32,48},{48,64},{64,80},{80,96},{96,112},{1,17},{17... | collective-permute-start | bytes 3128 | tf_op jit(solution)/shard_map/ppermute | solution.py:26
  18.1 26.2 %collective-permute-start.2 = (f32[2,1,130]{2,1,0:T(1,128)S(1)}, f32[2,1,130]{2,1,0:T(1,128)S(1)}, u32[]{:S(2)}, u32[]{:S(2)}) collective-permute-start(f32[2,1,130]{2,1,0:T(1,128)S(1)} %get-tuple-element.268), channel_id=1, source_target_pairs={{16,0},{32,16},{48,32},{64,48},{80,64},{96,80},{112,96},{17,1},{33... | collective-permute-start | bytes 3128 | tf_op jit(solution)/shard_map/ppermute | solution.py:29
  47.4 4.7 collective-permute-start.5
  52.1 25.7 %collective-permute-start.6 = (f32[1,1,130]{2,1,0:T(1,128)S(1)}, f32[1,1,130]{2,1,0:T(1,128)S(1)}, u32[]{:S(2)}, u32[]{:S(2)}) collective-permute-start(f32[1,1,130]{2,1,0:T(1,128)S(1)} %get-tuple-element.276), channel_id=1, source_target_pairs={{0,16},{16,32},{32,48},{48,64},{64,80},{80,96},{96,112},{1,17},{17... | collective-permute-start | bytes 1568 | tf_op jit(solution)/shard_map/ppermute | solution.py:26
  56.7 21.1 %collective-permute-start.7 = (f32[1,1,130]{2,1,0:T(1,128)S(1)}, f32[1,1,130]{2,1,0:T(1,128)S(1)}, u32[]{:S(2)}, u32[]{:S(2)}) collective-permute-start(f32[1,1,130]{2,1,0:T(1,128)S(1)} %get-tuple-element.277), channel_id=1, source_target_pairs={{16,0},{32,16},{48,32},{64,48},{80,64},{96,80},{112,96},{17,1},{33... | collective-permute-start | bytes 1568 | tf_op jit(solution)/shard_map/ppermute | solution.py:29
  78.1 8.4 %collective-permute-start.8 = (f32[2,32,1]{2,1,0:T(8,128)S(1)}, f32[2,32,1]{2,1,0:T(8,128)S(1)}, u32[]{:S(2)}, u32[]{:S(2)}) collective-permute-start(f32[2,32,1]{2,1,0:T(8,128)S(1)} %get-tuple-element.283), channel_id=1, source_target_pairs={{1,0},{2,1},{3,2},{4,3},{5,4},{6,5},{7,6},{8,7},{9,8},{10,9},{11,1... | collective-permute-start | bytes 776 | tf_op jit(solution)/shard_map/ppermute | solution.py:29
  78.5 8.0 %collective-permute-start.9 = (f32[2,32,1]{2,1,0:T(8,128)S(1)}, f32[2,32,1]{2,1,0:T(8,128)S(1)}, u32[]{:S(2)}, u32[]{:S(2)}) collective-permute-start(f32[2,32,1]{2,1,0:T(8,128)S(1)} %get-tuple-element.282), channel_id=1, source_target_pairs={{0,1},{1,2},{2,3},{3,4},{4,5},{5,6},{6,7},{7,8},{8,9},{9,10},{10,1... | collective-permute-start | bytes 776 | tf_op jit(solution)/shard_map/ppermute | solution.py:26
  81.4 155.5 %collective-permute-start.34 = (f32[9,1,130]{2,1,0:T(1,128)}, f32[9,1,130]{2,1,0:T(1,128)S(1)}, u32[]{:S(2)}, u32[]{:S(2)}) collective-permute-start(f32[9,1,130]{2,1,0:T(1,128)} %get-tuple-element.258), channel_id=1, source_target_pairs={{0,16},{16,32},{32,48},{48,64},{64,80},{80,96},{96,112},{1,17},{17... | collective-permute-start | bytes 14048 | tf_op jit(solution)/shard_map/ppermute | solution.py:26
  86.6 25.9 %collective-permute-start.11 = (f32[2,1,130]{2,1,0:T(1,128)S(1)}, f32[2,1,130]{2,1,0:T(1,128)S(1)}, u32[]{:S(2)}, u32[]{:S(2)}) collective-permute-start(f32[2,1,130]{2,1,0:T(1,128)S(1)} %get-tuple-element.267), channel_id=1, source_target_pairs={{0,16},{16,32},{32,48},{48,64},{64,80},{80,96},{96,112},{1,17},{17... | collective-permute-start | bytes 3128 | tf_op jit(solution)/shard_map/ppermute | solution.py:26
  90.3 22.2 %collective-permute-start.10 = (f32[2,1,130]{2,1,0:T(1,128)S(1)}, f32[2,1,130]{2,1,0:T(1,128)S(1)}, u32[]{:S(2)}, u32[]{:S(2)}) collective-permute-start(f32[2,1,130]{2,1,0:T(1,128)S(1)} %get-tuple-element.266), channel_id=1, source_target_pairs={{16,0},{32,16},{48,32},{64,48},{80,64},{96,80},{112,96},{17,1},{33... | collective-permute-start | bytes 3128 | tf_op jit(solution)/shard_map/ppermute | solution.py:29
  115.9 4.7 collective-permute-start.13
  120.7 25.3 %collective-permute-start.14 = (f32[1,1,130]{2,1,0:T(1,128)S(1)}, f32[1,1,130]{2,1,0:T(1,128)S(1)}, u32[]{:S(2)}, u32[]{:S(2)}) collective-permute-start(f32[1,1,130]{2,1,0:T(1,128)S(1)} %get-tuple-element.274), channel_id=1, source_target_pairs={{0,16},{16,32},{32,48},{48,64},{64,80},{80,96},{96,112},{1,17},{17... | collective-permute-start | bytes 1568 | tf_op jit(solution)/shard_map/ppermute | solution.py:26
  125.2 20.8 %collective-permute-start.15 = (f32[1,1,130]{2,1,0:T(1,128)S(1)}, f32[1,1,130]{2,1,0:T(1,128)S(1)}, u32[]{:S(2)}, u32[]{:S(2)}) collective-permute-start(f32[1,1,130]{2,1,0:T(1,128)S(1)} %get-tuple-element.275), channel_id=1, source_target_pairs={{16,0},{32,16},{48,32},{64,48},{80,64},{96,80},{112,96},{17,1},{33... | collective-permute-start | bytes 1568 | tf_op jit(solution)/shard_map/ppermute | solution.py:29
  146.3 23.1 %collective-permute-start.16 = (f32[2,32,1]{2,1,0:T(8,128)S(1)}, f32[2,32,1]{2,1,0:T(8,128)S(1)}, u32[]{:S(2)}, u32[]{:S(2)}) collective-permute-start(f32[2,32,1]{2,1,0:T(8,128)S(1)} %get-tuple-element.281), channel_id=1, source_target_pairs={{1,0},{2,1},{3,2},{4,3},{5,4},{6,5},{7,6},{8,7},{9,8},{10,9},{11,1... | collective-permute-start | bytes 776 | tf_op jit(solution)/shard_map/ppermute | solution.py:29
  146.6 22.7 %collective-permute-start.17 = (f32[2,32,1]{2,1,0:T(8,128)S(1)}, f32[2,32,1]{2,1,0:T(8,128)S(1)}, u32[]{:S(2)}, u32[]{:S(2)}) collective-permute-start(f32[2,32,1]{2,1,0:T(8,128)S(1)} %get-tuple-element.280), channel_id=1, source_target_pairs={{0,1},{1,2},{2,3},{3,4},{4,5},{5,6},{6,7},{7,8},{8,9},{9,10},{10,1... | collective-permute-start | bytes 776 | tf_op jit(solution)/shard_map/ppermute | solution.py:26
  169.5 29.0 %collective-permute-start.19 = (f32[2,1,130]{2,1,0:T(1,128)S(1)}, f32[2,1,130]{2,1,0:T(1,128)}, u32[]{:S(2)}, u32[]{:S(2)}) collective-permute-start(f32[2,1,130]{2,1,0:T(1,128)S(1)} %get-tuple-element.265), channel_id=1, source_target_pairs={{0,16},{16,32},{32,48},{48,64},{64,80},{80,96},{96,112},{1,17},{17... | collective-permute-start | bytes 3128 | tf_op jit(solution)/shard_map/ppermute | solution.py:26
  175.8 22.6 %collective-permute-start.18 = (f32[2,1,130]{2,1,0:T(1,128)S(1)}, f32[2,1,130]{2,1,0:T(1,128)S(1)}, u32[]{:S(2)}, u32[]{:S(2)}) collective-permute-start(f32[2,1,130]{2,1,0:T(1,128)S(1)} %get-tuple-element.264), channel_id=1, source_target_pairs={{16,0},{32,16},{48,32},{64,48},{80,64},{96,80},{112,96},{17,1},{33... | collective-permute-start | bytes 3128 | tf_op jit(solution)/shard_map/ppermute | solution.py:29
  200.8 5.0 collective-permute-start.21
  200.8 31.8 %collective-permute-start.35 = (f32[9,1,130]{2,1,0:T(1,128)}, f32[9,1,130]{2,1,0:T(1,128)S(1)}, u32[]{:S(2)}, u32[]{:S(2)}) collective-permute-start(f32[9,1,130]{2,1,0:T(1,128)} %get-tuple-element.259), channel_id=1, source_target_pairs={{16,0},{32,16},{48,32},{64,48},{80,64},{96,80},{112,96},{17,1},{33... | collective-permute-start | bytes 14048 | tf_op jit(solution)/shard_map/ppermute | solution.py:29
  205.8 26.8 %collective-permute-start.22 = (f32[1,1,130]{2,1,0:T(1,128)S(1)}, f32[1,1,130]{2,1,0:T(1,128)S(1)}, u32[]{:S(2)}, u32[]{:S(2)}) collective-permute-start(f32[1,1,130]{2,1,0:T(1,128)S(1)} %get-tuple-element.272), channel_id=1, source_target_pairs={{0,16},{16,32},{32,48},{48,64},{64,80},{80,96},{96,112},{1,17},{17... | collective-permute-start | bytes 1568 | tf_op jit(solution)/shard_map/ppermute | solution.py:26
  210.4 22.3 %collective-permute-start.23 = (f32[1,1,130]{2,1,0:T(1,128)S(1)}, f32[1,1,130]{2,1,0:T(1,128)S(1)}, u32[]{:S(2)}, u32[]{:S(2)}) collective-permute-start(f32[1,1,130]{2,1,0:T(1,128)S(1)} %get-tuple-element.273), channel_id=1, source_target_pairs={{16,0},{32,16},{48,32},{64,48},{80,64},{96,80},{112,96},{17,1},{33... | collective-permute-start | bytes 1568 | tf_op jit(solution)/shard_map/ppermute | solution.py:29
  233.6 4.9 collective-permute-start.24
  238.6 32.1 %collective-permute-start.27 = (f32[2,1,130]{2,1,0:T(1,128)S(1)}, f32[2,1,130]{2,1,0:T(1,128)S(1)}, u32[]{:S(2)}, u32[]{:S(2)}) collective-permute-start(f32[2,1,130]{2,1,0:T(1,128)S(1)} %get-tuple-element.263), channel_id=1, source_target_pairs={{0,16},{16,32},{32,48},{48,64},{64,80},{80,96},{96,112},{1,17},{17... | collective-permute-start | bytes 3128 | tf_op jit(solution)/shard_map/ppermute | solution.py:26
  245.2 25.4 %collective-permute-start.26 = (f32[2,1,130]{2,1,0:T(1,128)S(1)}, f32[2,1,130]{2,1,0:T(1,128)S(1)}, u32[]{:S(2)}, u32[]{:S(2)}) collective-permute-start(f32[2,1,130]{2,1,0:T(1,128)S(1)} %get-tuple-element.262), channel_id=1, source_target_pairs={{16,0},{32,16},{48,32},{64,48},{80,64},{96,80},{112,96},{17,1},{33... | collective-permute-start | bytes 3128 | tf_op jit(solution)/shard_map/ppermute | solution.py:29
  274.1 4.7 collective-permute-start.29
  280.1 30.2 %collective-permute-start.30 = (f32[1,1,130]{2,1,0:T(1,128)}, f32[1,1,130]{2,1,0:T(1,128)}, u32[]{:S(2)}, u32[]{:S(2)}) collective-permute-start(f32[1,1,130]{2,1,0:T(1,128)} %get-tuple-element.270), channel_id=1, source_target_pairs={{0,16},{16,32},{32,48},{48,64},{64,80},{80,96},{96,112},{1,17},{17... | collective-permute-start | bytes 1568 | tf_op jit(solution)/shard_map/ppermute | solution.py:26
  289.4 21.0 %collective-permute-start.31 = (f32[1,1,130]{2,1,0:T(1,128)}, f32[1,1,130]{2,1,0:T(1,128)S(1)}, u32[]{:S(2)}, u32[]{:S(2)}) collective-permute-start(f32[1,1,130]{2,1,0:T(1,128)} %get-tuple-element.271), channel_id=1, source_target_pairs={{16,0},{32,16},{48,32},{64,48},{80,64},{96,80},{112,96},{17,1},{33... | collective-permute-start | bytes 1568 | tf_op jit(solution)/shard_map/ppermute | solution.py:29
  382.2 45.0 %all-to-all-start = ((f32[4,128,1024]{2,0,1:T(4,128)}), f32[4,128,1024]{2,0,1:T(4,128)S(1)}, u32[]{:S(2)}, u32[]{:S(2)}) async-start(f32[4,128,1024]{2,0,1:T(4,128)} %copy.26), calls=%async_computation | async-start | bytes 4194304 | tf_op jit(solution)/shard_map/all_to_all | solution.py:180
  (21 other events, 1184.8 us)
where the time goes:
time: 559 us; the launch traced here: 557 us
  blocking collectives  191 us (34%)
  matrix products  139 us (25%)
  starting transfers between devices  97 us (17%)
  other arithmetic  59.9 us (11%)
  waiting for transfers between devices  45.9 us (8%)
  local copies, waits for them, and re-layouts  21.1 us (4%)
    all_gather x9, blocking collectives, widen(): collected = lax.all_gather(upper[None], 'lon', axis=0, tiled=True)  191 us
    dot_general x16, matrix products, add_block(): lax.dot_general(weighted, low_hot, (((0,), (0,)), ((), ())), precision=la...  79.6 us
    ppermute x18, starting transfers between devices, with_halo(): lax.ppermute(lax.slice_in_dim(block, block.shape[dim] - width, None, axis...  66.6 us
    dot_general x16, matrix products, one_block(): jnp.dot(column_hot, table, precision=lax.Precision.HIGHEST, preferred_ele...  59.5 us
    mul x16, other arithmetic, add_block(): jnp.transpose(value_block)[:, :, None] * high_hot[:, None, :]  39.1 us
    all_to_all x1, waiting for transfers between devices, local(): lax.all_to_all(values, ('lat', 'lon'), split_axis=1, concat_axis=1, tiled...  29 us
    ppermute x18, waiting for transfers between devices, with_halo(): lax.ppermute(lax.slice_in_dim(block, 0, width, axis=dim), axis, backward)  15.9 us
    ppermute x18, starting transfers between devices, with_halo(): lax.ppermute(lax.slice_in_dim(block, 0, width, axis=dim), axis, backward)  15.6 us
  transfers between devices with their start and end apart: 37, of which 8 were waited for; matrix products, arithmetic and copies ran while one was open for 3% of the time, Pallas kernels for 0%

commit v1 on v0

--- a/solution.py
+++ b/solution.py
@@ -37,7 +37,15 @@
     both_wide = with_halo(lon_wide, (("lat", 1),), width, False)
     upper = jnp.flip(lon_wide[:, rows - width :, :], axis=(1, 2))
     sectors = lax.axis_size("lon")
-    collected = lax.all_gather(upper[None], "lon", axis=0, tiled=True)
+    collected = jnp.concatenate(
+        lax.all_to_all(
+            jnp.stack([upper[None]] * lax.axis_size("lon"), axis=0),
+            concat_axis=0,
+            axis_name="lon",
+            split_axis=0,
+        ),
+        axis=0,
+    )
     mirrored = lax.dynamic_index_in_dim(
         collected, sectors - 1 - lax.axis_index("lon"), 0, keepdims=False
     )

time: 559 us -> 484 us (0.87)
  blocking collectives: 191 us -> 0 us
  starting transfers between devices: 97 us -> 184 us
  local copies, waits for them, and re-layouts: 21.1 us -> 39.6 us
  waiting for transfers between devices: 45.9 us -> 61.8 us
  other arithmetic: 59.9 us -> 54 us
    all_gather x9 -> x0, blocking collectives: 191 us -> none  [widen(): collected = lax.all_gather(upper[None], 'lon', axis=0, tiled=True)]
    all_to_all x0 -> x9, starting transfers between devices: none -> 70 us  [widen(): lax.all_to_all(jnp.stack([upper[None]] * lax.axis_size('lon'), axis=0), c...]
    dynamic_slice x32, local copies, waits for them, and re-layouts: 0.98 us -> 16.2 us  [pick_cells(): picked = lax.map(one_block, blocks).reshape(total, fields_count)]
    ppermute x18, starting transfers between devices: 66.6 us -> 80.5 us  [with_halo(): lax.ppermute(lax.slice_in_dim(block, block.shape[dim] - width, None, axis...]
    all_to_all x0 -> x9, waiting for transfers between devices: none -> 9.73 us  [widen(): lax.all_to_all(jnp.stack([upper[None]] * lax.axis_size('lon'), axis=0), c...]
    another operation x0 -> x9, local copies, waits for them, and re-layouts: none -> 5.78 us  [widen(): jnp.stack([upper[None]] * lax.axis_size('lon'), axis=0)]
    ppermute x18, waiting for transfers between devices: 0.96 us -> 6.66 us  [with_halo(): lax.ppermute(lax.slice_in_dim(block, block.shape[dim] - width, None, axis...]
  transfers between devices with their start and end apart: 37 -> 46, of which waited for: 8 -> 21; matrix products, arithmetic and copies ran while one was open for 3% -> 3% of each run, Pallas kernels for 0% -> 0%
where the time goes in v1:
time: 484 us; the launch traced here: 482 us
  starting transfers between devices  184 us (38%)
  matrix products  139 us (29%)
  waiting for transfers between devices  61.8 us (13%)
  other arithmetic  54 us (11%)
  local copies, waits for them, and re-layouts  39.6 us (8%)
    ppermute x18, starting transfers between devices, with_halo(): lax.ppermute(lax.slice_in_dim(block, block.shape[dim] - width, None, axis...  80.5 us
    dot_general x16, matrix products, add_block(): lax.dot_general(weighted, low_hot, (((0,), (0,)), ((), ())), precision=la...  79.6 us
    all_to_all x9, starting transfers between devices, widen(): lax.all_to_all(jnp.stack([upper[None]] * lax.axis_size('lon'), axis=0), c...  70 us
    dot_general x16, matrix products, one_block(): jnp.dot(column_hot, table, precision=lax.Precision.HIGHEST, preferred_ele...  59.5 us
    mul x16, other arithmetic, add_block(): jnp.transpose(value_block)[:, :, None] * high_hot[:, None, :]  39.8 us
    all_to_all x1, waiting for transfers between devices, local(): lax.all_to_all(values, ('lat', 'lon'), split_axis=1, concat_axis=1, tiled...  28.4 us
    all_to_all x1, starting transfers between devices, local(): lax.all_to_all(values, ('lat', 'lon'), split_axis=1, concat_axis=1, tiled...  19 us
    ppermute x18, waiting for transfers between devices, with_halo(): lax.ppermute(lax.slice_in_dim(block, 0, width, axis=dim), axis, backward)  17 us
  transfers between devices with their start and end apart: 46, of which 21 were waited for; matrix products, arithmetic and copies ran while one was open for 3% of the time, Pallas kernels for 0%

profile of v1, /device:TPU:1, one launch (start us, length us, event | category | flops | bytes accessed | tf_op | source)
XLA Modules:
  0.0 481.6 jit_solution(2303744628994002233)
XLA Ops:
  10.3 9.5 %all-to-all-start = ((f32[16,1,2,1,130]{4,3,2,1,0:T(1,128)}), f32[16,1,2,1,130]{4,3,2,1,0:T(1,128)S(1)}, u32[]{:S(2)}, u32[]{:S(2)}) async-start(f32[16,1,2,1,130]{4,3,2,1,0:T(1,128)} %stack.70), calls=%async_computation | async-start | bytes 65536 | tf_op jit(solution)/shard_map/all_to_all | solution.py:41
  36.6 6.3 %all-to-all-start.1 = ((f32[16,1,1,1,130]{4,3,2,1,0:T(1,128)}), f32[16,1,1,1,130]{4,3,2,1,0:T(1,128)S(1)}, u32[]{:S(2)}, u32[]{:S(2)}) async-start(f32[16,1,1,1,130]{4,3,2,1,0:T(1,128)} %stack.71), calls=%async_computation.1 | async-start | bytes 32768 | tf_op jit(solution)/shard_map/all_to_all | solution.py:41
  57.3 9.5 %all-to-all-start.2 = ((f32[16,1,2,1,130]{4,3,2,1,0:T(1,128)}), f32[16,1,2,1,130]{4,3,2,1,0:T(1,128)S(1)}, u32[]{:S(2)}, u32[]{:S(2)}) async-start(f32[16,1,2,1,130]{4,3,2,1,0:T(1,128)} %stack.75), calls=%async_computation.2 | async-start | bytes 65536 | tf_op jit(solution)/shard_map/all_to_all | solution.py:41
  87.3 7.7 %all-to-all-start.3 = ((f32[16,1,1,1,130]{4,3,2,1,0:T(1,128)}), f32[16,1,1,1,130]{4,3,2,1,0:T(1,128)S(1)}, u32[]{:S(2)}, u32[]{:S(2)}) async-start(f32[16,1,1,1,130]{4,3,2,1,0:T(1,128)} %stack.76), calls=%async_computation.3 | async-start | bytes 32768 | tf_op jit(solution)/shard_map/all_to_all | solution.py:41
  96.2 5.5 %collective-permute-start.14 = (f32[1,1,130]{2,1,0:T(1,128)S(1)}, f32[1,1,130]{2,1,0:T(1,128)S(1)}, u32[]{:S(2)}, u32[]{:S(2)}) collective-permute-start(f32[1,1,130]{2,1,0:T(1,128)S(1)} %get-tuple-element.298), channel_id=1, source_target_pairs={{0,16},{16,32},{32,48},{48,64},{64,80},{80,96},{96,112},{1,17},{17... | collective-permute-start | bytes 1568 | tf_op jit(solution)/shard_map/ppermute | solution.py:26
  109.9 9.5 %all-to-all-start.4 = ((f32[16,1,2,1,130]{4,3,2,1,0:T(1,128)}), f32[16,1,2,1,130]{4,3,2,1,0:T(1,128)S(1)}, u32[]{:S(2)}, u32[]{:S(2)}) async-start(f32[16,1,2,1,130]{4,3,2,1,0:T(1,128)} %stack.80), calls=%async_computation.4 | async-start | bytes 65536 | tf_op jit(solution)/shard_map/all_to_all | solution.py:41
  120.8 7.2 %collective-permute-start.34 = (f32[9,1,130]{2,0,1:T(8,128)S(1)}, f32[9,1,130]{2,0,1:T(8,128)S(1)}, u32[]{:S(2)}, u32[]{:S(2)}) collective-permute-start(f32[9,1,130]{2,0,1:T(8,128)S(1)} %get-tuple-element.282), channel_id=1, source_target_pairs={{0,16},{16,32},{32,48},{48,64},{64,80},{80,96},{96,112},{1,17},{17... | collective-permute-start | bytes 14048 | tf_op jit(solution)/shard_map/ppermute | solution.py:26
  128.0 5.8 %collective-permute-start.19 = (f32[2,1,130]{2,1,0:T(1,128)S(1)}, f32[2,1,130]{2,1,0:T(1,128)S(1)}, u32[]{:S(2)}, u32[]{:S(2)}) collective-permute-start(f32[2,1,130]{2,1,0:T(1,128)S(1)} %get-tuple-element.289), channel_id=1, source_target_pairs={{0,16},{16,32},{32,48},{48,64},{64,80},{80,96},{96,112},{1,17},{17... | collective-permute-start | bytes 3128 | tf_op jit(solution)/shard_map/ppermute | solution.py:26
  144.6 5.9 %all-to-all-start.5 = ((f32[16,1,1,1,130]{4,3,2,1,0:T(1,128)}), f32[16,1,1,1,130]{4,3,2,1,0:T(1,128)S(1)}, u32[]{:S(2)}, u32[]{:S(2)}) async-start(f32[16,1,1,1,130]{4,3,2,1,0:T(1,128)} %stack.81), calls=%async_computation.5 | async-start | bytes 32768 | tf_op jit(solution)/shard_map/all_to_all | solution.py:41
  153.2 7.9 %collective-permute-start.22 = (f32[1,1,130]{2,1,0:T(1,128)S(1)}, f32[1,1,130]{2,1,0:T(1,128)S(1)}, u32[]{:S(2)}, u32[]{:S(2)}) collective-permute-start(f32[1,1,130]{2,1,0:T(1,128)S(1)} %get-tuple-element.296), channel_id=1, source_target_pairs={{0,16},{16,32},{32,48},{48,64},{64,80},{80,96},{96,112},{1,17},{17... | collective-permute-start | bytes 1568 | tf_op jit(solution)/shard_map/ppermute | solution.py:26
  161.8 7.5 %all-to-all-start.8 = ((f32[16,1,9,1,130]{4,3,2,1,0:T(1,128)}), f32[16,1,9,1,130]{4,3,2,1,0:T(1,128)S(1)}, u32[]{:S(2)}, u32[]{:S(2)}) async-start(f32[16,1,9,1,130]{4,3,2,1,0:T(1,128)} %stack.87), calls=%async_computation.8 | async-start | bytes 294912 | tf_op jit(solution)/shard_map/all_to_all | solution.py:41
  178.2 8.1 %all-to-all-start.6 = ((f32[16,1,2,1,130]{4,3,2,1,0:T(1,128)}), f32[16,1,2,1,130]{4,3,2,1,0:T(1,128)S(1)}, u32[]{:S(2)}, u32[]{:S(2)}) async-start(f32[16,1,2,1,130]{4,3,2,1,0:T(1,128)} %stack.85), calls=%async_computation.6 | async-start | bytes 65536 | tf_op jit(solution)/shard_map/all_to_all | solution.py:41
  187.7 6.4 %collective-permute-start.27 = (f32[2,1,130]{2,1,0:T(1,128)S(1)}, f32[2,1,130]{2,1,0:T(1,128)S(1)}, u32[]{:S(2)}, u32[]{:S(2)}) collective-permute-start(f32[2,1,130]{2,1,0:T(1,128)S(1)} %get-tuple-element.287), channel_id=1, source_target_pairs={{0,16},{16,32},{32,48},{48,64},{64,80},{80,96},{96,112},{1,17},{17... | collective-permute-start | bytes 3128 | tf_op jit(solution)/shard_map/ppermute | solution.py:26
  204.7 5.9 %all-to-all-start.7 = ((f32[16,1,1,1,130]{4,3,2,1,0:T(1,128)}), f32[16,1,1,1,130]{4,3,2,1,0:T(1,128)S(1)}, u32[]{:S(2)}, u32[]{:S(2)}) async-start(f32[16,1,1,1,130]{4,3,2,1,0:T(1,128)} %stack.86), calls=%async_computation.7 | async-start | bytes 32768 | tf_op jit(solution)/shard_map/all_to_all | solution.py:41
  219.7 78.1 %while.26 = (s32[]{:T(128)}, f32[16,8192,4]{1,2,0:T(4,128)S(1)}, s32[16,8192]{1,0:T(8,128)}, f32[128,128]{1,0:T(8,128)S(1)}, s32[]{:T(128)}) while((s32[]{:T(128)}, f32[16,8192,4]{1,2,0:T(4,128)S(1)}, s32[16,8192]{1,0:T(8,128)}, f32[128,128]{1,0:T(8,128)S(1)}, s32[]{:T(128)}) %tuple.101), condition=%wide.region_2.3_spmd.clone, body=%wide.region_0.2_spmd.clone.sunk | while | flops 1614405632 | bytes 2785349 | solution.py:76
  301.8 19.0 %all-to-all-start.9 = ((f32[4,128,1024]{2,0,1:T(4,128)}), f32[4,128,1024]{2,0,1:T(4,128)S(1)}, u32[]{:S(2)}, u32[]{:S(2)}) async-start(f32[4,128,1024]{2,0,1:T(4,128)} %copy.50), calls=%async_computation.9 | async-start | bytes 4194304 | tf_op jit(solution)/shard_map/all_to_all | solution.py:188
  322.7 28.4 %all-to-all-done.9 = f32[4,128,1024]{2,0,1:T(4,128)S(1)} async-done(((f32[4,128,1024]{2,0,1:T(4,128)}), f32[4,128,1024]{2,0,1:T(4,128)S(1)}, u32[]{:S(2)}, u32[]{:S(2)}) %all-to-all-start.9) | async-done | bytes 2097184 | tf_op jit(solution)/shard_map/all_to_all | solution.py:188
  355.3 125.6 %while.27 = (s32[]{:T(128)}, f32[128,128]{1,0:T(8,128)S(1)}, f32[16,4,8192]{2,0,1:T(8,128)S(1)}, s32[16,8192]{1,0:T(8,128)S(1)}, s32[]{:T(128)}, /*index=5*/s32[]{:T(128)}) while((s32[]{:T(128)}, f32[128,128]{1,0:T(8,128)S(1)}, f32[16,4,8192]{2,0,1:T(8,128)S(1)}, s32[16,8192]{1,0:T(8,128)S(1)}, s32[]{:T(128)}, ...), condition=%wide.region_4.5_spmd.clone, body=%wide.region_3.4_spmd.clone.sunk | while | flops 1613422592 | bytes 11501655 | solution.py:107
  358.2 5.0 %fusion.120 = f32[128,128]{1,0:T(8,128)S(1)} fusion(f32[8192,128]{0,1:T(8,128)} %bitcast.157, s32[8192]{0:T(1024)S(1)} %get-tuple-element.375, f32[128,128]{1,0:T(8,128)S(1)} %get-tuple-element.398, pred[]{:T(512)S(6)} %compare.31), kind=kOutput, calls=%fused_computation.24.clone.1 | convolution fusion | flops 1611694080 | bytes 4358145 | tf_op jit(solution)/shard_map/while/body/eval_jaxpr/dot_general | solution.py:97
  366.0 5.0 %fusion.120 = f32[128,128]{1,0:T(8,128)S(1)} fusion(f32[8192,128]{0,1:T(8,128)} %bitcast.157, s32[8192]{0:T(1024)S(1)} %get-tuple-element.375, f32[128,128]{1,0:T(8,128)S(1)} %get-tuple-element.398, pred[]{:T(512)S(6)} %compare.31), kind=kOutput, calls=%fused_computation.24.clone.1 | convolution fusion | flops 1611694080 | bytes 4358145 | tf_op jit(solution)/shard_map/while/body/eval_jaxpr/dot_general | solution.py:97
  373.9 5.0 %fusion.120 = f32[128,128]{1,0:T(8,128)S(1)} fusion(f32[8192,128]{0,1:T(8,128)} %bitcast.157, s32[8192]{0:T(1024)S(1)} %get-tuple-element.375, f32[128,128]{1,0:T(8,128)S(1)} %get-tuple-element.398, pred[]{:T(512)S(6)} %compare.31), kind=kOutput, calls=%fused_computation.24.clone.1 | convolution fusion | flops 1611694080 | bytes 4358145 | tf_op jit(solution)/shard_map/while/body/eval_jaxpr/dot_general | solution.py:97
  381.7 5.0 %fusion.120 = f32[128,128]{1,0:T(8,128)S(1)} fusion(f32[8192,128]{0,1:T(8,128)} %bitcast.157, s32[8192]{0:T(1024)S(1)} %get-tuple-element.375, f32[128,128]{1,0:T(8,128)S(1)} %get-tuple-element.398, pred[]{:T(512)S(6)} %compare.31), kind=kOutput, calls=%fused_computation.24.clone.1 | convolution fusion | flops 1611694080 | bytes 4358145 | tf_op jit(solution)/shard_map/while/body/eval_jaxpr/dot_general | solution.py:97
  389.6 5.0 %fusion.120 = f32[128,128]{1,0:T(8,128)S(1)} fusion(f32[8192,128]{0,1:T(8,128)} %bitcast.157, s32[8192]{0:T(1024)S(1)} %get-tuple-element.375, f32[128,128]{1,0:T(8,128)S(1)} %get-tuple-element.398, pred[]{:T(512)S(6)} %compare.31), kind=kOutput, calls=%fused_computation.24.clone.1 | convolution fusion | flops 1611694080 | bytes 4358145 | tf_op jit(solution)/shard_map/while/body/eval_jaxpr/dot_general | solution.py:97
  397.4 5.0 %fusion.120 = f32[128,128]{1,0:T(8,128)S(1)} fusion(f32[8192,128]{0,1:T(8,128)} %bitcast.157, s32[8192]{0:T(1024)S(1)} %get-tuple-element.375, f32[128,128]{1,0:T(8,128)S(1)} %get-tuple-element.398, pred[]{:T(512)S(6)} %compare.31), kind=kOutput, calls=%fused_computation.24.clone.1 | convolution fusion | flops 1611694080 | bytes 4358145 | tf_op jit(solution)/shard_map/while/body/eval_jaxpr/dot_general | solution.py:97
  405.3 5.0 %fusion.120 = f32[128,128]{1,0:T(8,128)S(1)} fusion(f32[8192,128]{0,1:T(8,128)} %bitcast.157, s32[8192]{0:T(1024)S(1)} %get-tuple-element.375, f32[128,128]{1,0:T(8,128)S(1)} %get-tuple-element.398, pred[]{:T(512)S(6)} %compare.31), kind=kOutput, calls=%fused_computation.24.clone.1 | convolution fusion | flops 1611694080 | bytes 4358145 | tf_op jit(solution)/shard_map/while/body/eval_jaxpr/dot_general | solution.py:97
  413.1 5.0 %fusion.120 = f32[128,128]{1,0:T(8,128)S(1)} fusion(f32[8192,128]{0,1:T(8,128)} %bitcast.157, s32[8192]{0:T(1024)S(1)} %get-tuple-element.375, f32[128,128]{1,0:T(8,128)S(1)} %get-tuple-element.398, pred[]{:T(512)S(6)} %compare.31), kind=kOutput, calls=%fused_computation.24.clone.1 | convolution fusion | flops 1611694080 | bytes 4358145 | tf_op jit(solution)/shard_map/while/body/eval_jaxpr/dot_general | solution.py:97
  421.0 5.0 %fusion.120 = f32[128,128]{1,0:T(8,128)S(1)} fusion(f32[8192,128]{0,1:T(8,128)} %bitcast.157, s32[8192]{0:T(1024)S(1)} %get-tuple-element.375, f32[128,128]{1,0:T(8,128)S(1)} %get-tuple-element.398, pred[]{:T(512)S(6)} %compare.31), kind=kOutput, calls=%fused_computation.24.clone.1 | convolution fusion | flops 1611694080 | bytes 4358145 | tf_op jit(solution)/shard_map/while/body/eval_jaxpr/dot_general | solution.py:97
  428.8 5.0 %fusion.120 = f32[128,128]{1,0:T(8,128)S(1)} fusion(f32[8192,128]{0,1:T(8,128)} %bitcast.157, s32[8192]{0:T(1024)S(1)} %get-tuple-element.375, f32[128,128]{1,0:T(8,128)S(1)} %get-tuple-element.398, pred[]{:T(512)S(6)} %compare.31), kind=kOutput, calls=%fused_computation.24.clone.1 | convolution fusion | flops 1611694080 | bytes 4358145 | tf_op jit(solution)/shard_map/while/body/eval_jaxpr/dot_general | solution.py:97
  436.7 5.0 %fusion.120 = f32[128,128]{1,0:T(8,128)S(1)} fusion(f32[8192,128]{0,1:T(8,128)} %bitcast.157, s32[8192]{0:T(1024)S(1)} %get-tuple-element.375, f32[128,128]{1,0:T(8,128)S(1)} %get-tuple-element.398, pred[]{:T(512)S(6)} %compare.31), kind=kOutput, calls=%fused_computation.24.clone.1 | convolution fusion | flops 1611694080 | bytes 4358145 | tf_op jit(solution)/shard_map/while/body/eval_jaxpr/dot_general | solution.py:97
  444.5 5.0 %fusion.120 = f32[128,128]{1,0:T(8,128)S(1)} fusion(f32[8192,128]{0,1:T(8,128)} %bitcast.157, s32[8192]{0:T(1024)S(1)} %get-tuple-element.375, f32[128,128]{1,0:T(8,128)S(1)} %get-tuple-element.398, pred[]{:T(512)S(6)} %compare.31), kind=kOutput, calls=%fused_computation.24.clone.1 | convolution fusion | flops 1611694080 | bytes 4358145 | tf_op jit(solution)/shard_map/while/body/eval_jaxpr/dot_general | solution.py:97
  452.4 5.0 %fusion.120 = f32[128,128]{1,0:T(8,128)S(1)} fusion(f32[8192,128]{0,1:T(8,128)} %bitcast.157, s32[8192]{0:T(1024)S(1)} %get-tuple-element.375, f32[128,128]{1,0:T(8,128)S(1)} %get-tuple-element.398, pred[]{:T(512)S(6)} %compare.31), kind=kOutput, calls=%fused_computation.24.clone.1 | convolution fusion | flops 1611694080 | bytes 4358145 | tf_op jit(solution)/shard_map/while/body/eval_jaxpr/dot_general | solution.py:97
  460.2 5.0 %fusion.120 = f32[128,128]{1,0:T(8,128)S(1)} fusion(f32[8192,128]{0,1:T(8,128)} %bitcast.157, s32[8192]{0:T(1024)S(1)} %get-tuple-element.375, f32[128,128]{1,0:T(8,128)S(1)} %get-tuple-element.398, pred[]{:T(512)S(6)} %compare.31), kind=kOutput, calls=%fused_computation.24.clone.1 | convolution fusion | flops 1611694080 | bytes 4358145 | tf_op jit(solution)/shard_map/while/body/eval_jaxpr/dot_general | solution.py:97
  (366 shorter events, 258.6 us)
Async XLA Ops:
  2.2 5.9 %collective-permute-start = (f32[2,32,1]{2,1,0:T(8,128)S(1)}, f32[2,32,1]{2,1,0:T(8,128)S(1)}, u32[]{:S(2)}, u32[]{:S(2)}) collective-permute-start(f32[2,32,1]{2,1,0:T(8,128)S(1)} %get-tuple-element.309), channel_id=1, source_target_pairs={{1,0},{2,1},{3,2},{4,3},{5,4},{6,5},{7,6},{8,7},{9,8},{10,9},{11,1... | collective-permute-start | bytes 776 | tf_op jit(solution)/shard_map/ppermute | solution.py:29
  3.6 5.6 %collective-permute-start.1 = (f32[2,32,1]{2,1,0:T(8,128)S(1)}, f32[2,32,1]{2,1,0:T(8,128)S(1)}, u32[]{:S(2)}, u32[]{:S(2)}) collective-permute-start(f32[2,32,1]{2,1,0:T(8,128)S(1)} %get-tuple-element.308), channel_id=1, source_target_pairs={{0,1},{1,2},{2,3},{3,4},{4,5},{5,6},{6,7},{7,8},{8,9},{9,10},{10,1... | collective-permute-start | bytes 776 | tf_op jit(solution)/shard_map/ppermute | solution.py:26
  10.3 16.9 %all-to-all-start = ((f32[16,1,2,1,130]{4,3,2,1,0:T(1,128)}), f32[16,1,2,1,130]{4,3,2,1,0:T(1,128)S(1)}, u32[]{:S(2)}, u32[]{:S(2)}) async-start(f32[16,1,2,1,130]{4,3,2,1,0:T(1,128)} %stack.70), calls=%async_computation | async-start | bytes 65536 | tf_op jit(solution)/shard_map/all_to_all | solution.py:41
  21.1 6.1 %collective-permute-start.3 = (f32[2,1,130]{2,1,0:T(1,128)S(1)}, f32[2,1,130]{2,1,0:T(1,128)S(1)}, u32[]{:S(2)}, u32[]{:S(2)}) collective-permute-start(f32[2,1,130]{2,1,0:T(1,128)S(1)} %get-tuple-element.293), channel_id=1, source_target_pairs={{0,16},{16,32},{32,48},{48,64},{64,80},{80,96},{96,112},{1,17},{17... | collective-permute-start | bytes 3128 | tf_op jit(solution)/shard_map/ppermute | solution.py:26
  36.6 13.6 %all-to-all-start.1 = ((f32[16,1,1,1,130]{4,3,2,1,0:T(1,128)}), f32[16,1,1,1,130]{4,3,2,1,0:T(1,128)S(1)}, u32[]{:S(2)}, u32[]{:S(2)}) async-start(f32[16,1,1,1,130]{4,3,2,1,0:T(1,128)} %stack.71), calls=%async_computation.1 | async-start | bytes 32768 | tf_op jit(solution)/shard_map/all_to_all | solution.py:41
  44.2 6.0 %collective-permute-start.6 = (f32[1,1,130]{2,1,0:T(1,128)S(1)}, f32[1,1,130]{2,1,0:T(1,128)S(1)}, u32[]{:S(2)}, u32[]{:S(2)}) collective-permute-start(f32[1,1,130]{2,1,0:T(1,128)S(1)} %get-tuple-element.300), channel_id=1, source_target_pairs={{0,16},{16,32},{32,48},{48,64},{64,80},{80,96},{96,112},{1,17},{17... | collective-permute-start | bytes 1568 | tf_op jit(solution)/shard_map/ppermute | solution.py:26
  57.3 19.1 %all-to-all-start.2 = ((f32[16,1,2,1,130]{4,3,2,1,0:T(1,128)}), f32[16,1,2,1,130]{4,3,2,1,0:T(1,128)S(1)}, u32[]{:S(2)}, u32[]{:S(2)}) async-start(f32[16,1,2,1,130]{4,3,2,1,0:T(1,128)} %stack.75), calls=%async_computation.2 | async-start | bytes 65536 | tf_op jit(solution)/shard_map/all_to_all | solution.py:41
  66.8 9.6 %collective-permute-start.10 = (f32[2,1,130]{2,1,0:T(1,128)S(1)}, f32[2,1,130]{2,1,0:T(1,128)S(1)}, u32[]{:S(2)}, u32[]{:S(2)}) collective-permute-start(f32[2,1,130]{2,1,0:T(1,128)S(1)} %get-tuple-element.290), channel_id=1, source_target_pairs={{16,0},{32,16},{48,32},{64,48},{80,64},{96,80},{112,96},{17,1},{33... | collective-permute-start | bytes 3128 | tf_op jit(solution)/shard_map/ppermute | solution.py:29
  69.0 51.7 %collective-permute-start.32 = (f32[9,32,1]{2,0,1:T(8,128)}, f32[9,32,1]{2,0,1:T(8,128)S(1)}, u32[]{:S(2)}, u32[]{:S(2)}) collective-permute-start(f32[9,32,1]{2,0,1:T(8,128)} %get-tuple-element.284), channel_id=1, source_target_pairs={{0,1},{1,2},{2,3},{3,4},{4,5},{5,6},{6,7},{7,8},{8,9},{9,10},{10,1... | collective-permute-start | bytes 3464 | tf_op jit(solution)/shard_map/ppermute | solution.py:26
  72.1 48.6 %collective-permute-start.33 = (f32[9,32,1]{2,0,1:T(8,128)}, f32[9,32,1]{2,0,1:T(8,128)S(1)}, u32[]{:S(2)}, u32[]{:S(2)}) collective-permute-start(f32[9,32,1]{2,0,1:T(8,128)} %get-tuple-element.285), channel_id=1, source_target_pairs={{1,0},{2,1},{3,2},{4,3},{5,4},{6,5},{7,6},{8,7},{9,8},{10,9},{11,1... | collective-permute-start | bytes 3464 | tf_op jit(solution)/shard_map/ppermute | solution.py:29
  87.3 15.0 %all-to-all-start.3 = ((f32[16,1,1,1,130]{4,3,2,1,0:T(1,128)}), f32[16,1,1,1,130]{4,3,2,1,0:T(1,128)S(1)}, u32[]{:S(2)}, u32[]{:S(2)}) async-start(f32[16,1,1,1,130]{4,3,2,1,0:T(1,128)} %stack.76), calls=%async_computation.3 | async-start | bytes 32768 | tf_op jit(solution)/shard_map/all_to_all | solution.py:41
  95.0 6.8 %collective-permute-start.15 = (f32[1,1,130]{2,1,0:T(1,128)S(1)}, f32[1,1,130]{2,1,0:T(1,128)S(1)}, u32[]{:S(2)}, u32[]{:S(2)}) collective-permute-start(f32[1,1,130]{2,1,0:T(1,128)S(1)} %get-tuple-element.299), channel_id=1, source_target_pairs={{16,0},{32,16},{48,32},{64,48},{80,64},{96,80},{112,96},{17,1},{33... | collective-permute-start | bytes 1568 | tf_op jit(solution)/shard_map/ppermute | solution.py:29
  96.2 6.2 %collective-permute-start.14 = (f32[1,1,130]{2,1,0:T(1,128)S(1)}, f32[1,1,130]{2,1,0:T(1,128)S(1)}, u32[]{:S(2)}, u32[]{:S(2)}) collective-permute-start(f32[1,1,130]{2,1,0:T(1,128)S(1)} %get-tuple-element.298), channel_id=1, source_target_pairs={{0,16},{16,32},{32,48},{48,64},{64,80},{80,96},{96,112},{1,17},{17... | collective-permute-start | bytes 1568 | tf_op jit(solution)/shard_map/ppermute | solution.py:26
  102.8 6.0 %collective-permute-start.16 = (f32[2,32,1]{2,1,0:T(8,128)S(1)}, f32[2,32,1]{2,1,0:T(8,128)S(1)}, u32[]{:S(2)}, u32[]{:S(2)}) collective-permute-start(f32[2,32,1]{2,1,0:T(8,128)S(1)} %get-tuple-element.305), channel_id=1, source_target_pairs={{1,0},{2,1},{3,2},{4,3},{5,4},{6,5},{7,6},{8,7},{9,8},{10,9},{11,1... | collective-permute-start | bytes 776 | tf_op jit(solution)/shard_map/ppermute | solution.py:29
  109.9 24.0 %all-to-all-start.4 = ((f32[16,1,2,1,130]{4,3,2,1,0:T(1,128)}), f32[16,1,2,1,130]{4,3,2,1,0:T(1,128)S(1)}, u32[]{:S(2)}, u32[]{:S(2)}) async-start(f32[16,1,2,1,130]{4,3,2,1,0:T(1,128)} %stack.80), calls=%async_computation.4 | async-start | bytes 65536 | tf_op jit(solution)/shard_map/all_to_all | solution.py:41
  119.4 14.4 %collective-permute-start.18 = (f32[2,1,130]{2,1,0:T(1,128)S(1)}, f32[2,1,130]{2,1,0:T(1,128)S(1)}, u32[]{:S(2)}, u32[]{:S(2)}) collective-permute-start(f32[2,1,130]{2,1,0:T(1,128)S(1)} %get-tuple-element.288), channel_id=1, source_target_pairs={{16,0},{32,16},{48,32},{64,48},{80,64},{96,80},{112,96},{17,1},{33... | collective-permute-start | bytes 3128 | tf_op jit(solution)/shard_map/ppermute | solution.py:29
  120.8 66.8 %collective-permute-start.34 = (f32[9,1,130]{2,0,1:T(8,128)S(1)}, f32[9,1,130]{2,0,1:T(8,128)S(1)}, u32[]{:S(2)}, u32[]{:S(2)}) collective-permute-start(f32[9,1,130]{2,0,1:T(8,128)S(1)} %get-tuple-element.282), channel_id=1, source_target_pairs={{0,16},{16,32},{32,48},{48,64},{64,80},{80,96},{96,112},{1,17},{17... | collective-permute-start | bytes 14048 | tf_op jit(solution)/shard_map/ppermute | solution.py:26
  128.0 6.5 %collective-permute-start.19 = (f32[2,1,130]{2,1,0:T(1,128)S(1)}, f32[2,1,130]{2,1,0:T(1,128)S(1)}, u32[]{:S(2)}, u32[]{:S(2)}) collective-permute-start(f32[2,1,130]{2,1,0:T(1,128)S(1)} %get-tuple-element.289), channel_id=1, source_target_pairs={{0,16},{16,32},{32,48},{48,64},{64,80},{80,96},{96,112},{1,17},{17... | collective-permute-start | bytes 3128 | tf_op jit(solution)/shard_map/ppermute | solution.py:26
  144.6 16.5 %all-to-all-start.5 = ((f32[16,1,1,1,130]{4,3,2,1,0:T(1,128)}), f32[16,1,1,1,130]{4,3,2,1,0:T(1,128)S(1)}, u32[]{:S(2)}, u32[]{:S(2)}) async-start(f32[16,1,1,1,130]{4,3,2,1,0:T(1,128)} %stack.81), calls=%async_computation.5 | async-start | bytes 32768 | tf_op jit(solution)/shard_map/all_to_all | solution.py:41
  150.6 18.8 %collective-permute-start.23 = (f32[1,1,130]{2,1,0:T(1,128)S(1)}, f32[1,1,130]{2,1,0:T(1,128)S(1)}, u32[]{:S(2)}, u32[]{:S(2)}) collective-permute-start(f32[1,1,130]{2,1,0:T(1,128)S(1)} %get-tuple-element.297), channel_id=1, source_target_pairs={{16,0},{32,16},{48,32},{64,48},{80,64},{96,80},{112,96},{17,1},{33... | collective-permute-start | bytes 1568 | tf_op jit(solution)/shard_map/ppermute | solution.py:29
  151.9 25.2 %collective-permute-start.35 = (f32[9,1,130]{2,0,1:T(8,128)S(1)}, f32[9,1,130]{2,0,1:T(8,128)S(1)}, u32[]{:S(2)}, u32[]{:S(2)}) collective-permute-start(f32[9,1,130]{2,0,1:T(8,128)S(1)} %get-tuple-element.283), channel_id=1, source_target_pairs={{16,0},{32,16},{48,32},{64,48},{80,64},{96,80},{112,96},{17,1},{33... | collective-permute-start | bytes 14048 | tf_op jit(solution)/shard_map/ppermute | solution.py:29
  153.2 16.2 %collective-permute-start.22 = (f32[1,1,130]{2,1,0:T(1,128)S(1)}, f32[1,1,130]{2,1,0:T(1,128)S(1)}, u32[]{:S(2)}, u32[]{:S(2)}) collective-permute-start(f32[1,1,130]{2,1,0:T(1,128)S(1)} %get-tuple-element.296), channel_id=1, source_target_pairs={{0,16},{16,32},{32,48},{48,64},{64,80},{80,96},{96,112},{1,17},{17... | collective-permute-start | bytes 1568 | tf_op jit(solution)/shard_map/ppermute | solution.py:26
  161.8 15.3 %all-to-all-start.8 = ((f32[16,1,9,1,130]{4,3,2,1,0:T(1,128)}), f32[16,1,9,1,130]{4,3,2,1,0:T(1,128)S(1)}, u32[]{:S(2)}, u32[]{:S(2)}) async-start(f32[16,1,9,1,130]{4,3,2,1,0:T(1,128)} %stack.87), calls=%async_computation.8 | async-start | bytes 294912 | tf_op jit(solution)/shard_map/all_to_all | solution.py:41
  169.6 7.5 %collective-permute-start.24 = (f32[2,32,1]{2,1,0:T(8,128)S(1)}, f32[2,32,1]{2,1,0:T(8,128)S(1)}, u32[]{:S(2)}, u32[]{:S(2)}) collective-permute-start(f32[2,32,1]{2,1,0:T(8,128)S(1)} %get-tuple-element.303), channel_id=1, source_target_pairs={{1,0},{2,1},{3,2},{4,3},{5,4},{6,5},{7,6},{8,7},{9,8},{10,9},{11,1... | collective-permute-start | bytes 776 | tf_op jit(solution)/shard_map/ppermute | solution.py:29
  169.8 7.4 %collective-permute-start.25 = (f32[2,32,1]{2,1,0:T(8,128)S(1)}, f32[2,32,1]{2,1,0:T(8,128)S(1)}, u32[]{:S(2)}, u32[]{:S(2)}) collective-permute-start(f32[2,32,1]{2,1,0:T(8,128)S(1)} %get-tuple-element.302), channel_id=1, source_target_pairs={{0,1},{1,2},{2,3},{3,4},{4,5},{5,6},{6,7},{7,8},{8,9},{9,10},{10,1... | collective-permute-start | bytes 776 | tf_op jit(solution)/shard_map/ppermute | solution.py:26
  178.2 16.0 %all-to-all-start.6 = ((f32[16,1,2,1,130]{4,3,2,1,0:T(1,128)}), f32[16,1,2,1,130]{4,3,2,1,0:T(1,128)S(1)}, u32[]{:S(2)}, u32[]{:S(2)}) async-start(f32[16,1,2,1,130]{4,3,2,1,0:T(1,128)} %stack.85), calls=%async_computation.6 | async-start | bytes 65536 | tf_op jit(solution)/shard_map/all_to_all | solution.py:41
  186.3 7.9 %collective-permute-start.26 = (f32[2,1,130]{2,1,0:T(1,128)S(1)}, f32[2,1,130]{2,1,0:T(1,128)S(1)}, u32[]{:S(2)}, u32[]{:S(2)}) collective-permute-start(f32[2,1,130]{2,1,0:T(1,128)S(1)} %get-tuple-element.286), channel_id=1, source_target_pairs={{16,0},{32,16},{48,32},{64,48},{80,64},{96,80},{112,96},{17,1},{33... | collective-permute-start | bytes 3128 | tf_op jit(solution)/shard_map/ppermute | solution.py:29
  187.7 7.1 %collective-permute-start.27 = (f32[2,1,130]{2,1,0:T(1,128)S(1)}, f32[2,1,130]{2,1,0:T(1,128)S(1)}, u32[]{:S(2)}, u32[]{:S(2)}) collective-permute-start(f32[2,1,130]{2,1,0:T(1,128)S(1)} %get-tuple-element.287), channel_id=1, source_target_pairs={{0,16},{16,32},{32,48},{48,64},{64,80},{80,96},{96,112},{1,17},{17... | collective-permute-start | bytes 3128 | tf_op jit(solution)/shard_map/ppermute | solution.py:26
  204.7 13.2 %all-to-all-start.7 = ((f32[16,1,1,1,130]{4,3,2,1,0:T(1,128)}), f32[16,1,1,1,130]{4,3,2,1,0:T(1,128)S(1)}, u32[]{:S(2)}, u32[]{:S(2)}) async-start(f32[16,1,1,1,130]{4,3,2,1,0:T(1,128)} %stack.86), calls=%async_computation.7 | async-start | bytes 32768 | tf_op jit(solution)/shard_map/all_to_all | solution.py:41
  210.6 5.9 %collective-permute-start.31 = (f32[1,1,130]{2,1,0:T(1,128)S(1)}, f32[1,1,130]{2,1,0:T(1,128)S(1)}, u32[]{:S(2)}, u32[]{:S(2)}) collective-permute-start(f32[1,1,130]{2,1,0:T(1,128)S(1)} %get-tuple-element.295), channel_id=1, source_target_pairs={{16,0},{32,16},{48,32},{64,48},{80,64},{96,80},{112,96},{17,1},{33... | collective-permute-start | bytes 1568 | tf_op jit(solution)/shard_map/ppermute | solution.py:29
  212.0 5.9 %collective-permute-start.30 = (f32[1,1,130]{2,1,0:T(1,128)S(1)}, f32[1,1,130]{2,1,0:T(1,128)S(1)}, u32[]{:S(2)}, u32[]{:S(2)}) collective-permute-start(f32[1,1,130]{2,1,0:T(1,128)S(1)} %get-tuple-element.294), channel_id=1, source_target_pairs={{0,16},{16,32},{32,48},{48,64},{64,80},{80,96},{96,112},{1,17},{17... | collective-permute-start | bytes 1568 | tf_op jit(solution)/shard_map/ppermute | solution.py:26
  301.8 49.2 %all-to-all-start.9 = ((f32[4,128,1024]{2,0,1:T(4,128)}), f32[4,128,1024]{2,0,1:T(4,128)S(1)}, u32[]{:S(2)}, u32[]{:S(2)}) async-start(f32[4,128,1024]{2,0,1:T(4,128)} %copy.50), calls=%async_computation.9 | async-start | bytes 4194304 | tf_op jit(solution)/shard_map/all_to_all | solution.py:188
  (21 other events, 466.5 us)
